TPU v7x, 512 devices: a whole 4x8x8 slice. The times are simulated.
512 devices in a mesh: ctx: 64 (over z, y), chan: 4 (over x), phase: 2 (over core).
Axes of the slice: x: 4, y: 8, z: 8, core: 2. Of those that a mesh axis runs over, the one named last changes fastest.
Arguments:
- projected: bfloat16 [2, 3, 16384, 8192], P('phase', None, 'ctx', 'chan'), may hold values from -6 to 6
- short_filter: float32 [2, 3, 3, 8192], P('phase', None, None, 'chan'), may hold values from -3.5 to 3.5
- decay_rate: float32 [2, 64, 16], P('phase', 'chan'), may hold values from 1.8310547e-05 to 0.08, as said below
- residue: float32 [2, 64, 16], P('phase', 'chan'), may hold values from -0.25980762 to 0.25980762
- norm_gain: float32 [2, 8192], P('phase', 'chan'), may hold values from 0.1 to 1.9
- lengths: int32 [2, 4], P('phase'), may hold values from 1 to 6144, 16384 in all within a row
Outputs:
- handoff: bfloat16 [2, 16384, 8192], P('phase', 'ctx', 'chan')
Inputs may be any that keep to these rules, and one draw needn't show every extreme that they name: Each row holds 4 sequence lengths, two preference pairs (chosen, then rejected), that sum to 16384; the longest is exactly 6144. `decay_rate`: positive decay rates.
All inputs are finite; a program needn't handle non-finite values.
Results may differ from a plain program's by a relative error of at most 0.0061.
Values may be sent and summed in bfloat16 or wider, within the bound.
No kernel may reach another device: no remote copies, remote signals or barrier semaphores. Data moves between devices by JAX's collectives and lax.ppermute only.
A program may use at most 64 MiB of HBM per device.

v0:
```python
import jax
import jax.numpy as jnp
from jax import lax
from jax.sharding import PartitionSpec as P

D = 8192
GW = 128
SHORT = 3


EPSILON = 1e-05


def from_behind(shard, axis, by):
    length = lax.axis_size(axis)
    pairs = [(i, i + by) for i in range(length) if 0 <= i + by < length]
    return lax.ppermute(shard, axis, pairs)


def from_behind_2(value, axis, steps):
    count = lax.axis_size(axis)
    pairs = [(source, (source + steps) % count) for source in range(count)]
    return lax.ppermute(value, axis, pairs)


def segment_starts(seq_lengths, positions):
    starts = jnp.cumsum(seq_lengths) - seq_lengths
    chosen = jnp.where(starts[None, :] <= positions[:, None], starts[None, :], 0)
    return jnp.max(chosen, axis=1)


def lag_kernel(pole_rate, residue_here, block_len):
    row_index = jnp.arange(block_len, dtype=jnp.int32)
    lag_steps = row_index[:, None] - row_index[None, :]
    causal = lag_steps >= 0
    lag_float = jnp.maximum(lag_steps, 0).astype(jnp.float32)
    summed = jnp.zeros((pole_rate.shape[0], block_len, block_len), jnp.float32)
    for mode_index in range(pole_rate.shape[1]):
        summed = summed + residue_here[:, mode_index, None, None] * jnp.exp(
            -pole_rate[:, mode_index, None, None] * lag_float[None]
        )
    return jnp.where(causal[None], summed, 0.0).astype(jnp.bfloat16)


def join_states(earlier, later):
    return (earlier[0] * later[0], later[0][..., None] * earlier[1] + later[1])


def by_channel(gated_prod, pole_rate, residue_here, seq_lengths, ctx_count, ctx_pos):
    tok_dev, width_here = gated_prod.shape
    highest = lax.Precision.HIGHEST
    part_width = width_here // ctx_count
    gathered = lax.all_to_all(gated_prod.T, "ctx", split_axis=0, concat_axis=1, tiled=True)
    all_tokens = tok_dev * ctx_count
    group_count = max(1, part_width // GW)
    per_group = part_width // group_count
    first_group = ctx_pos * part_width // GW
    rate_part = lax.dynamic_slice_in_dim(pole_rate, first_group, group_count, 0)
    residue_part = lax.dynamic_slice_in_dim(residue_here, first_group, group_count, 0)
    starts = segment_starts(seq_lengths, jnp.arange(all_tokens, dtype=jnp.int32)).reshape(
        ctx_count, tok_dev
    )
    within = jnp.arange(tok_dev, dtype=jnp.int32)
    anchors = jnp.arange(ctx_count, dtype=jnp.int32) * tok_dev
    global_pos = anchors[:, None] + within[None, :]
    values = gathered.reshape(group_count, per_group, ctx_count, tok_dev)
    kernel = lag_kernel(rate_part, residue_part, tok_dev)
    inside = (within[None, None, :] <= within[None, :, None]) & (
        global_pos[:, None, :] >= starts[:, :, None]
    )
    masked = jnp.where(inside[:, None], kernel[None], jnp.zeros((), jnp.bfloat16))
    intra_term = jnp.einsum("bgts,gcbs->gcbt", masked, values, preferred_element_type=jnp.float32)
    last_start = starts[:, tok_dev - 1]
    kept_rows = (global_pos >= last_start[:, None]).astype(jnp.float32)
    fading = (
        jnp.exp(
            -rate_part[None, None] * (tok_dev - 1 - within)[None, :, None, None].astype(jnp.float32)
        )
        * kept_rows[:, :, None, None]
    )
    fresh_state = jnp.einsum(
        "bsgm,gcbs->bgmc", fading, values.astype(jnp.float32), precision=highest
    )
    through = jnp.where(
        (last_start < anchors)[:, None, None], jnp.exp(-rate_part * tok_dev)[None], 0.0
    )
    inclusive = lax.associative_scan(join_states, (through, fresh_state), axis=0)
    prior_state = jnp.concatenate([jnp.zeros_like(fresh_state[:1]), inclusive[1][:-1]], axis=0)
    carry_rows = (starts < anchors[:, None]).astype(jnp.float32)
    reaching = (
        residue_part[None, None]
        * jnp.exp(-rate_part[None, None] * (within + 1)[None, :, None, None].astype(jnp.float32))
        * carry_rows[:, :, None, None]
    )
    inter_term = jnp.einsum("btgm,bgmc->gcbt", reaching, prior_state, precision=highest)
    mixed_conv = (
        (intra_term + inter_term).astype(jnp.bfloat16).reshape(part_width, ctx_count, tok_dev)
    )
    returned = lax.all_to_all(mixed_conv, "ctx", split_axis=1, concat_axis=0, tiled=True)
    return returned.reshape(width_here, tok_dev).T


def on_device(projected, short_filter, decay_rate, residue, norm_gain, lengths):
    features = projected[0]
    filters = short_filter[0]
    pole_rate = decay_rate[0]
    residue_here = residue[0]
    seq_lengths = lengths[0]
    tok_dev = features.shape[1]
    width_here = features.shape[2]
    ctx_count = lax.axis_size("ctx")
    ctx_pos = lax.axis_index("ctx")
    anchor = ctx_pos * tok_dev
    positions = anchor + jnp.arange(tok_dev, dtype=jnp.int32)
    starts = segment_starts(seq_lengths, positions)
    rim_rows = from_behind(features[:, tok_dev - (SHORT - 1) :, :], "ctx", 1)
    extended = jnp.concatenate([rim_rows, features], axis=1)
    short_out = jnp.zeros((3, tok_dev, width_here), jnp.float32)
    for tap_index in range(SHORT):
        shifted = extended[:, SHORT - 1 - tap_index : SHORT - 1 - tap_index + tok_dev]
        usable = (positions - tap_index >= starts).astype(jnp.float32)
        short_out = (
            short_out
            + filters[:, tap_index, None, :] * shifted.astype(jnp.float32) * usable[None, :, None]
        )
    gated_prod = (short_out[1] * short_out[2]).astype(jnp.bfloat16)
    mixed_conv = by_channel(gated_prod, pole_rate, residue_here, seq_lengths, ctx_count, ctx_pos)
    activity = short_out[0] * mixed_conv.astype(jnp.float32)
    squares = lax.psum(jnp.sum(activity * activity, axis=1), "chan")
    normed = (activity * lax.rsqrt(squares[:, None] / D + EPSILON) * norm_gain[0][None, :]).astype(
        jnp.bfloat16
    )
    handoff = from_behind_2(normed, "phase", 1)
    return handoff[None]


def solution(mesh):
    in_specs = (
        P("phase", None, "ctx", "chan"),
        P("phase", None, None, "chan"),
        P("phase", "chan", None),
        P("phase", "chan", None),
        P("phase", "chan"),
        P("phase", None),
    )
    out_specs = P("phase", "ctx", "chan")
    return jax.shard_map(
        on_device, mesh=mesh, in_specs=in_specs, out_specs=out_specs, check_vma=False
    )
```

profile of v0, /device:TPU:1, one launch (start us, length us, event | category | flops | bytes accessed | tf_op | source)
XLA Modules:
  0.0 131.6 jit_solution(2476134335035197759)
XLA Ops:
  0.0 0.9 slice.359
  0.9 4.0 %collective-permute-start = (bf16[3,2,2048]{2,1,0:T(2,128)(2,1)S(1)}, bf16[3,2,2048]{2,1,0:T(2,128)(2,1)S(1)}, u32[]{:S(2)}, u32[]{:S(2)}) collective-permute-start(bf16[3,2,2048]{2,1,0:T(2,128)(2,1)S(1)} %slice.359), channel_id=1, source_target_pairs={{0,8},{8,16},{16,24},{24,32},{32,40},{40,48},{48,56},{56,64},{64,7... | collective-permute-start | bytes 73736 | tf_op jit(solution)/shard_map/ppermute | solution.py:17
  5.0 0.8 reduce-window_clone.1
  5.8 0.7 subtract_bitcast_fusion
  6.4 0.4 select_reduce_fusion
  6.9 0.2 slice_reduce_fusion
  7.1 0.9 copy.27
  8.2 6.4 %multiply_add_fusion = f32[3,256,2048]{2,1,0:T(8,128)S(1)} fusion(bf16[3,256,2048]{2,1,0:T(8,128)(2,1)} %bitcast.116, bf16[3,2,2048]{2,1,0:T(2,128)(2,1)S(1)} %collective-permute-done, f32[256]{0:T(256)S(1)} %get-tuple-element.18, f32[3,2048]{1,0:T(4,128)S(1)} %get-tuple-element.58, f32[256]{0:T(256)S(1)} %get-tuple-element.19, ...), kind=kLoop, calls=%fused_computation.5 | loop fusion | flops 26738688 | bytes 9538560 | tf_op jit(solution)/shard_map/add | solution.py:123
  14.6 2.7 %copy-done = f32[3,256,2048]{2,1,0:T(8,128)} copy-done((f32[3,256,2048]{2,1,0:T(8,128)}, f32[3,256,2048]{2,1,0:T(8,128)S(1)}, u32[]{:S(2)}) %copy-start) | copy-done | bytes 6291480
  17.3 0.3 fusion.10
  17.5 1.3 copy.17
  18.8 15.6 %all-to-all-start = ((bf16[64,32,256]{2,1,0:T(8,128)(2,1)}), bf16[64,32,256]{2,1,0:T(8,128)(2,1)S(1)}, u32[]{:S(2)}, u32[]{:S(2)}) async-start(bf16[64,32,256]{2,1,0:T(8,128)(2,1)} %bitcast.5), calls=%async_computation | async-start | bytes 2097152 | tf_op jit(solution)/shard_map/all_to_all | solution.py:53
  34.4 0.7 exponential_bitcast_fusion
  35.5 0.7 fusion.40
  46.3 0.7 fusion.39
  47.0 10.6 %select_convert_fusion = bf16[256,256]{1,0:T(8,128)(2,1)S(1)} fusion(f32[]{:T(128)} %bitcast.40, f32[]{:T(128)} %bitcast.39, f32[]{:T(128)} %bitcast.38, f32[]{:T(128)} %bitcast.37, f32[]{:T(128)} %bitcast.36, f32[]{:T(128)} %bitcast.35, f32[]{:T(128)} %bitcast.34, f32[]{:T(128)} %bitcast.33, f32[]{:T(128)} %bitcast.32, f32[]{:T(128)} %bitcast.31, ...), kind=kLoop, calls=%fused_computation.35 | loop fusion | flops 3473408 | bytes 131200 | tf_op jit(solution)/shard_map/convert_element_type | solution.py:42
  57.9 2.4 %all-to-all-done = bf16[64,32,256]{2,1,0:T(8,128)(2,1)S(1)} async-done(((bf16[64,32,256]{2,1,0:T(8,128)(2,1)}), bf16[64,32,256]{2,1,0:T(8,128)(2,1)S(1)}, u32[]{:S(2)}, u32[]{:S(2)}) %all-to-all-start) | async-done | bytes 1048608 | tf_op jit(solution)/shard_map/all_to_all | solution.py:53
  60.3 0.9 fusion.11
  61.3 0.1 slice_add_fusion
  63.1 0.3 pad.65
  63.4 0.3 pad.101
  63.7 2.9 %fusion = f32[64,32,256]{2,1,0:T(8,128)S(1)} fusion(s32[64,256]{1,0:T(8,128)S(1)} %ge.62, s32[64,256]{1,0:T(8,128)S(1)} %iota_add_fusion, pred[256,256]{1,0:T(8,128)(4,1)S(1)} %iota_compare_fusion.1, bf16[256,256]{1,0:T(8,128)(2,1)S(1)} %select_convert_fusion, bf16[64,32,256]{2,1,0:T(8,128)(2,1)S(1)} %all-to-all-done), kind=kOutput, calls=%fused_computation.1 | convolution fusion | flops 281018368 | bytes 3473408 | tf_op jit(solution)/shard_map/bgts,gcbs->gcbt/dot_general | solution.py:72
  66.6 2.0 %fusion.9 = bf16[32,64,256]{2,0,1:T(8,128)(2,1)S(1)} fusion(f32[64,32,256]{2,1,0:T(8,128)S(1)} %fusion, f32[64,256]{1,0:T(8,128)S(1)} %get-tuple-element.23, f32[256,16]{0,1:T(8,128)S(1)} %get-tuple-element.21, f32[63,1,16,32]{3,2,0,1:T(8,128)S(1)} %slice_add_fusion.6), kind=kOutput, calls=%fused_computation.19 | convolution fusion | flops 101974016 | bytes 3356672 | tf_op jit(solution)/shard_map/btgm,bgmc->gcbt/dot_general | solution.py:95
  68.6 35.2 %all_to_all.25 = bf16[32,64,256]{2,0,1:T(8,128)(2,1)S(1)} all-to-all(bf16[32,64,256]{2,0,1:T(8,128)(2,1)S(1)} %fusion.9), channel_id=1, replica_groups=mesh['ctx'=64,'chan'=4,'phase'=2] {'ctx'}, dimensions={1} | all-to-all | bytes 2097152 | tf_op jit(solution)/shard_map/all_to_all | solution.py:99
  103.9 1.6 %bitcast_convert_fusion = f32[32,64,1,256]{3,0,1,2:T(8,128)} fusion(bf16[32,64,256]{2,0,1:T(8,128)(2,1)S(1)} %all_to_all.25), kind=kLoop, calls=%fused_computation.21 | loop fusion | flops 524288 | bytes 3145728 | tf_op jit(solution)/shard_map/convert_element_type | solution.py:128
  105.5 1.9 %copy.18 = f32[2048,256]{0,1:T(8,128)S(1)} copy(f32[2048,256]{1,0:T(8,128)} %bitcast.112) | data formatting | bytes 4194304 | tf_op jit(solution)/shard_map/convert_element_type | solution.py:128
  107.4 1.9 %multiply_reduce_fusion = f32[256]{0:T(256)S(1)} fusion(f32[2048,256]{0,1:T(8,128)S(1)} %copy.18, f32[3,256,2048]{2,1,0:T(8,128)} %copy-done), kind=kLoop, calls=%fused_computation.17 | loop fusion | flops 1572608 | bytes 4195328 | tf_op jit(solution)/shard_map/reduce_sum | solution.py:129
  109.3 8.5 %psum.7 = f32[256]{0:T(256)S(1)} all-reduce(f32[256]{0:T(256)S(1)} %multiply_reduce_fusion), channel_id=1, replica_groups=mesh['ctx'=64,'chan'=4,'phase'=2] {'chan'}, use_global_device_ids=true, to_apply=%region_4.5 | all-reduce | flops 256 | bytes 2048 | tf_op jit(solution)/shard_map/psum | solution.py:129
  117.8 1.9 %multiply_convert_fusion = bf16[256,2048]{1,0:T(8,128)(2,1)S(1)} fusion(f32[2048]{0:T(1024)S(1)} %bitcast.128, f32[256]{0:T(256)S(1)} %add_rsqrt_fusion, f32[2048,256]{0,1:T(8,128)S(1)} %copy.18, f32[3,256,2048]{2,1,0:T(8,128)} %copy-done), kind=kLoop, calls=%fused_computation.16 | loop fusion | flops 2097152 | bytes 5252096 | tf_op jit(solution)/shard_map/convert_element_type | solution.py:130
  119.7 8.6 %collective-permute-start.1 = (bf16[256,2048]{1,0:T(8,128)(2,1)S(1)}, bf16[256,2048]{1,0:T(8,128)(2,1)S(1)}, u32[]{:S(2)}, u32[]{:S(2)}) collective-permute-start(bf16[256,2048]{1,0:T(8,128)(2,1)S(1)} %multiply_convert_fusion), channel_id=1, source_target_pairs={{0,1},{1,0},{2,3},{3,2},{4,5},{5,4},{6,7},{7,6},{8,9},{9,8},{10,11... | collective-permute-start | bytes 3145736 | tf_op jit(solution)/shard_map/ppermute | solution.py:23
  128.3 2.3 %collective-permute-done.1 = bf16[256,2048]{1,0:T(8,128)(2,1)S(1)} collective-permute-done((bf16[256,2048]{1,0:T(8,128)(2,1)S(1)}, bf16[256,2048]{1,0:T(8,128)(2,1)S(1)}, u32[]{:S(2)}, u32[]{:S(2)}) %collective-permute-start.1) | collective-permute-done | bytes 1048608 | tf_op jit(solution)/shard_map/ppermute | solution.py:23
  130.6 1.0 copy.30
  (74 shorter events, 2.4 us)
Async XLA Ops:
  0.9 7.3 %collective-permute-start = (bf16[3,2,2048]{2,1,0:T(2,128)(2,1)S(1)}, bf16[3,2,2048]{2,1,0:T(2,128)(2,1)S(1)}, u32[]{:S(2)}, u32[]{:S(2)}) collective-permute-start(bf16[3,2,2048]{2,1,0:T(2,128)(2,1)S(1)} %slice.359), channel_id=1, source_target_pairs={{0,8},{8,16},{16,24},{24,32},{32,40},{40,48},{48,56},{56,64},{64,7... | collective-permute-start | bytes 73736 | tf_op jit(solution)/shard_map/ppermute | solution.py:17
  14.6 2.7 %copy-start = (f32[3,256,2048]{2,1,0:T(8,128)}, f32[3,256,2048]{2,1,0:T(8,128)S(1)}, u32[]{:S(2)}) copy-start(f32[3,256,2048]{2,1,0:T(8,128)S(1)} %multiply_add_fusion) | copy-start | bytes 18874372
  18.8 41.5 %all-to-all-start = ((bf16[64,32,256]{2,1,0:T(8,128)(2,1)}), bf16[64,32,256]{2,1,0:T(8,128)(2,1)S(1)}, u32[]{:S(2)}, u32[]{:S(2)}) async-start(bf16[64,32,256]{2,1,0:T(8,128)(2,1)} %bitcast.5), calls=%async_computation | async-start | bytes 2097152 | tf_op jit(solution)/shard_map/all_to_all | solution.py:53
  103.9 13.9 %copy-start.1 = (f32[1,2048]{1,0:T(1,128)S(1)}, f32[1,2048]{1,0:T(1,128)}, u32[]{:S(2)}) copy-start(f32[1,2048]{1,0:T(1,128)} %param.10) | copy-start | bytes 24580
  119.7 10.9 %collective-permute-start.1 = (bf16[256,2048]{1,0:T(8,128)(2,1)S(1)}, bf16[256,2048]{1,0:T(8,128)(2,1)S(1)}, u32[]{:S(2)}, u32[]{:S(2)}) collective-permute-start(bf16[256,2048]{1,0:T(8,128)(2,1)S(1)} %multiply_convert_fusion), channel_id=1, source_target_pairs={{0,1},{1,0},{2,3},{3,2},{4,5},{5,4},{6,7},{7,6},{8,9},{9,8},{10,11... | collective-permute-start | bytes 3145736 | tf_op jit(solution)/shard_map/ppermute | solution.py:23
where the time goes:
time: 132 us
  blocking collectives  43.7 us (33%)
  starting transfers between devices  28.3 us (21%)
  other arithmetic  26.9 us (20%)
  local copies, waits for them, and re-layouts  11.7 us (9%)
  between operations  10.4 us (8%)
  matrix products  5.87 us (4%)
  waiting for transfers between devices  4.68 us (4%)
    all_to_all x1, blocking collectives, by_channel(): lax.all_to_all(mixed_conv, 'ctx', split_axis=1, concat_axis=0, tiled=True)  35.2 us
    all_to_all x1, starting transfers between devices, by_channel(): lax.all_to_all(gated_prod.T, 'ctx', split_axis=0, concat_axis=1, tiled=True)  15.6 us
    convert_element_type x1, other arithmetic, lag_kernel(): return jnp.where(causal[None], summed, 0.0).astype(jnp.bfloat16)  10.6 us
    ppermute x1, starting transfers between devices, from_behind_2(): return lax.ppermute(value, axis, pairs)  8.64 us
    psum x1, blocking collectives, on_device(): squares = lax.psum(jnp.sum(activity * activity, axis=1), 'chan')  8.47 us
    add x1, other arithmetic, on_device(): short_out + filters[:, tap_index, None, :] * shifted.astype(jnp.float32)...  6.37 us
    unnamed x9, local copies, waits for them, and re-layouts  4.86 us
    ppermute x1, starting transfers between devices, from_behind(): return lax.ppermute(shard, axis, pairs)  4.02 us
  transfers between devices with their start and end apart: 3, of which 2 were waited for; matrix products, arithmetic and copies ran while one was open for 13% of the time, Pallas kernels for 0%

commit v1 on v0

v1 whole, which is shorter than its diff:
```python
import jax
import jax.numpy as jnp
from jax import lax
from jax.sharding import PartitionSpec as P

GW = 128
SHORT = 3
LONGEST = 6144

EPSILON = 1e-05
HIGHEST = lax.Precision.HIGHEST


def from_behind(shard, axis, by):
    length = lax.axis_size(axis)
    pairs = [(i, i + by) for i in range(length) if 0 <= i + by < length]
    return lax.ppermute(shard, axis, pairs)


def from_behind_2(value, axis, steps):
    count = lax.axis_size(axis)
    pairs = [(source, (source + steps) % count) for source in range(count)]
    return lax.ppermute(value, axis, pairs)


def butterfly_sum(value, axis):
    count = lax.axis_size(axis)
    step = 1
    while step < count:
        pairs = [(i, i ^ step) for i in range(count)]
        value = value + lax.ppermute(value, axis, pairs)
        step *= 2
    return value


def segment_starts(seq_lengths, positions):
    starts = jnp.cumsum(seq_lengths) - seq_lengths
    chosen = jnp.where(starts[None, :] <= positions[:, None], starts[None, :], 0)
    return jnp.max(chosen, axis=1)


def prior_states(through, fresh, block_len):
    ctx_count = lax.axis_size("ctx")
    need = min(ctx_count, LONGEST // block_len + 1)
    decay = from_behind(through, "ctx", 1)
    state = from_behind(fresh, "ctx", 1)
    cover = 1
    while cover < need:
        decay_before = from_behind(decay, "ctx", cover)
        state_before = from_behind(state, "ctx", cover)
        state = decay[..., None] * state_before + state
        decay = decay * decay_before
        cover *= 2
    return state


def on_device(projected, short_filter, decay_rate, residue, norm_gain, lengths):
    features = projected[0]
    filters = short_filter[0]
    pole_rate = decay_rate[0]
    residue_here = residue[0]
    seq_lengths = lengths[0]
    tok_dev = features.shape[1]
    width_here = features.shape[2]
    group_count = width_here // GW
    full_width = width_here * lax.axis_size("chan")
    ctx_pos = lax.axis_index("ctx")
    anchor = ctx_pos * tok_dev
    within = jnp.arange(tok_dev, dtype=jnp.int32)
    positions = anchor + within
    starts = segment_starts(seq_lengths, positions)

    rim_rows = from_behind(features[:, tok_dev - (SHORT - 1) :, :], "ctx", 1)
    extended = jnp.concatenate([rim_rows, features], axis=1)
    short_out = jnp.zeros((3, tok_dev, width_here), jnp.float32)
    for tap_index in range(SHORT):
        shifted = extended[:, SHORT - 1 - tap_index : SHORT - 1 - tap_index + tok_dev]
        usable = (positions - tap_index >= starts).astype(jnp.float32)
        short_out = (
            short_out
            + filters[:, tap_index, None, :] * shifted.astype(jnp.float32) * usable[None, :, None]
        )
    gated_prod = (short_out[1] * short_out[2]).astype(jnp.bfloat16)
    values = gated_prod.reshape(tok_dev, group_count, GW)

    last_start = starts[tok_dev - 1]
    kept_rows = (positions >= last_start).astype(jnp.float32)
    fading = (
        jnp.exp(-pole_rate[None] * (tok_dev - 1 - within)[:, None, None].astype(jnp.float32))
        * kept_rows[:, None, None]
    )
    fresh_state = jnp.einsum(
        "sgm,sgc->gmc", fading, values.astype(jnp.float32), precision=HIGHEST
    )
    through = jnp.where(last_start < anchor, jnp.exp(-pole_rate * tok_dev), 0.0)
    prior_state = prior_states(through, fresh_state, tok_dev)

    middle = tok_dev // 2
    offsets = (within - middle).astype(jnp.float32)
    left = residue_here[:, None, :] * jnp.exp(-pole_rate[:, None, :] * offsets[None, :, None])
    right = jnp.exp(pole_rate[:, :, None] * offsets[None, None, :])
    summed = jnp.einsum("gtm,gms->gts", left, right, precision=HIGHEST)
    inside = (within[None, :] <= within[:, None]) & (positions[None, :] >= starts[:, None])
    masked = jnp.where(inside[None], summed, 0.0).astype(jnp.bfloat16)
    intra_term = jnp.einsum("gts,sgc->tgc", masked, values, preferred_element_type=jnp.float32)

    carry_rows = (starts < anchor).astype(jnp.float32)
    reaching = (
        residue_here[None]
        * jnp.exp(-pole_rate[None] * (within + 1)[:, None, None].astype(jnp.float32))
        * carry_rows[:, None, None]
    )
    inter_term = jnp.einsum("tgm,gmc->tgc", reaching, prior_state, precision=HIGHEST)
    mixed_conv = (intra_term + inter_term).astype(jnp.bfloat16).reshape(tok_dev, width_here)

    activity = short_out[0] * mixed_conv.astype(jnp.float32)
    squares = butterfly_sum(jnp.sum(activity * activity, axis=1), "chan")
    normed = (
        activity * lax.rsqrt(squares[:, None] / full_width + EPSILON) * norm_gain[0][None, :]
    ).astype(jnp.bfloat16)
    handoff = from_behind_2(normed, "phase", 1)
    return handoff[None]


def solution(mesh):
    in_specs = (
        P("phase", None, "ctx", "chan"),
        P("phase", None, None, "chan"),
        P("phase", "chan", None),
        P("phase", "chan", None),
        P("phase", "chan"),
        P("phase", None),
    )
    out_specs = P("phase", "ctx", "chan")
    return jax.shard_map(
        on_device, mesh=mesh, in_specs=in_specs, out_specs=out_specs, check_vma=False
    )
```

time: 132 us -> 125 us (0.947)
  starting transfers between devices: 28.3 us -> 82 us
  blocking collectives: 43.7 us -> 0 us
  other arithmetic: 26.9 us -> 14 us
  between operations: 10.4 us -> 1 us
  waiting for transfers between devices: 4.68 us -> 10.1 us
  local copies, waits for them, and re-layouts: 11.7 us -> 7.7 us
  matrix products: 5.87 us -> 9.02 us
    ppermute x1 -> x12, starting transfers between devices: 4.02 us -> 61.1 us  [from_behind(): return lax.ppermute(shard, axis, pairs)]
    all_to_all x1 -> x0, blocking collectives: 35.2 us -> none  [by_channel(): lax.all_to_all(mixed_conv, 'ctx', split_axis=1, concat_axis=0, tiled=True)]
    all_to_all x1 -> x0, starting transfers between devices: 15.6 us -> none  [by_channel(): lax.all_to_all(gated_prod.T, 'ctx', split_axis=0, concat_axis=1, tiled=True)]
    convert_element_type x6, other arithmetic: 14.2 us -> 2.57 us  [the longest x1 1.9 us: on_device(): normed = (activity * lax.rsqrt(squares[:, None] / full_width + EPSILON) *...]
    psum x1 -> x0, blocking collectives: 8.47 us -> none  [on_device(): squares = lax.psum(jnp.sum(activity * activity, axis=1), 'chan')]
    ppermute x0 -> x2, starting transfers between devices: none -> 7.75 us  [butterfly_sum(): value = value + lax.ppermute(value, axis, pairs)]
    ppermute x1 -> x12, waiting for transfers between devices: 0.01 us -> 5.47 us  [from_behind(): return lax.ppermute(shard, axis, pairs)]
    ppermute x1, starting transfers between devices: 8.64 us -> 13.2 us  [from_behind_2(): return lax.ppermute(value, axis, pairs)]
  transfers between devices with their start and end apart: 3 -> 15, of which waited for: 2 -> 9; matrix products, arithmetic and copies ran while one was open for 13% -> 8% of each run, Pallas kernels for 0% -> 0%
where the time goes in v1:
time: 125 us; the launch traced here: 124 us
  starting transfers between devices  82 us (66%)
  other arithmetic  14 us (11%)
  waiting for transfers between devices  10.1 us (8%)
  matrix products  9.02 us (7%)
  local copies, waits for them, and re-layouts  7.7 us (6%)
    ppermute x12, starting transfers between devices, from_behind(): return lax.ppermute(shard, axis, pairs)  61.1 us
    ppermute x1, starting transfers between devices, from_behind_2(): return lax.ppermute(value, axis, pairs)  13.2 us
    ppermute x2, starting transfers between devices, butterfly_sum(): value = value + lax.ppermute(value, axis, pairs)  7.75 us
    add x1, other arithmetic, on_device(): short_out + filters[:, tap_index, None, :] * shifted.astype(jnp.float32)...  6.37 us
    ppermute x12, waiting for transfers between devices, from_behind(): return lax.ppermute(shard, axis, pairs)  5.47 us
    unnamed x13, local copies, waits for them, and re-layouts  4.22 us
    dot_general x1, matrix products, on_device(): summed = jnp.einsum('gtm,gms->gts', left, right, precision=HIGHEST)  4.11 us
    dot_general x1, matrix products, on_device(): jnp.einsum('tgm,gmc->tgc', reaching, prior_state, precision=HIGHEST)  3.4 us
  transfers between devices with their start and end apart: 15, of which 9 were waited for; matrix products, arithmetic and copies ran while one was open for 8% of the time, Pallas kernels for 0%

profile of v1, /device:TPU:1, one launch (start us, length us, event | category | flops | bytes accessed | tf_op | source)
XLA Modules:
  0.0 123.8 jit_solution(5987820635928905251)
XLA Ops:
  0.0 0.9 slice.42
  0.9 4.0 %collective-permute-start = (bf16[3,2,2048]{2,1,0:T(2,128)(2,1)S(1)}, bf16[3,2,2048]{2,1,0:T(2,128)(2,1)S(1)}, u32[]{:S(2)}, u32[]{:S(2)}) collective-permute-start(bf16[3,2,2048]{2,1,0:T(2,128)(2,1)S(1)} %slice.42), channel_id=1, source_target_pairs={{0,8},{8,16},{16,24},{24,32},{32,40},{40,48},{48,56},{56,64},{64,7... | collective-permute-start | bytes 73736 | tf_op jit(solution)/shard_map/ppermute | solution.py:17
  5.0 0.8 reduce-window_clone.1
  7.1 0.9 copy.26
  9.6 6.4 %multiply_add_fusion = f32[3,256,2048]{2,1,0:T(8,128)S(1)} fusion(bf16[3,256,2048]{2,1,0:T(8,128)(2,1)} %bitcast.43, bf16[3,2,2048]{2,1,0:T(2,128)(2,1)S(1)} %collective-permute-done, f32[256]{0:T(256)S(1)} %get-tuple-element.11, f32[3,2048]{1,0:T(4,128)S(1)} %get-tuple-element.14, f32[256]{0:T(256)S(1)} %get-tuple-element.12, ...), kind=kLoop, calls=%fused_computation | loop fusion | flops 26738688 | bytes 9538560 | tf_op jit(solution)/shard_map/add | solution.py:80
  16.6 2.0 %copy-done = f32[3,256,2048]{2,1,0:T(8,128)} copy-done((f32[3,256,2048]{2,1,0:T(8,128)}, f32[3,256,2048]{2,1,0:T(8,128)S(1)}, u32[]{:S(2)}) %copy-start) | copy-done | bytes 6291480
  19.3 3.2 %collective-permute-start.6 = (f32[16,16,128]{2,1,0:T(8,128)S(1)}, f32[16,16,128]{2,1,0:T(8,128)S(1)}, u32[]{:S(2)}, u32[]{:S(2)}) collective-permute-start(f32[16,16,128]{2,1,0:T(8,128)S(1)} %fusion.7), channel_id=1, source_target_pairs={{0,8},{8,16},{16,24},{24,32},{32,40},{40,48},{48,56},{56,64},{64,7... | collective-permute-start | bytes 393224 | tf_op jit(solution)/shard_map/ppermute | solution.py:17
  23.1 1.3 %collective-permute-done.6 = f32[16,16,128]{2,1,0:T(8,128)S(1)} collective-permute-done((f32[16,16,128]{2,1,0:T(8,128)S(1)}, f32[16,16,128]{2,1,0:T(8,128)S(1)}, u32[]{:S(2)}, u32[]{:S(2)}) %collective-permute-start.6) | collective-permute-done | bytes 131104 | tf_op jit(solution)/shard_map/ppermute | solution.py:17
  24.4 3.8 %collective-permute-start.7 = (f32[16,16,128]{2,1,0:T(8,128)S(1)}, f32[16,16,128]{2,1,0:T(8,128)S(1)}, u32[]{:S(2)}, u32[]{:S(2)}) collective-permute-start(f32[16,16,128]{2,1,0:T(8,128)S(1)} %collective-permute-done.6), channel_id=1, source_target_pairs={{0,8},{8,16},{16,24},{24,32},{32,40},{40,48},{48,56},{56,64},{64,7... | collective-permute-start | bytes 393224 | tf_op jit(solution)/shard_map/ppermute | solution.py:17
  28.2 3.8 %collective-permute-start.1 = (f32[16,16]{1,0:T(8,128)S(1)}, f32[16,16]{1,0:T(8,128)S(1)}, u32[]{:S(2)}, u32[]{:S(2)}) collective-permute-start(f32[16,16]{1,0:T(8,128)S(1)} %get-tuple-element.8), channel_id=1, source_target_pairs={{0,8},{8,16},{16,24},{24,32},{32,40},{40,48},{48,56},{56,64},{64,7... | collective-permute-start | bytes 3080 | tf_op jit(solution)/shard_map/ppermute | solution.py:17
  32.9 5.3 %collective-permute-start.8 = (f32[16,16,128]{2,1,0:T(8,128)S(1)}, f32[16,16,128]{2,1,0:T(8,128)S(1)}, u32[]{:S(2)}, u32[]{:S(2)}) collective-permute-start(f32[16,16,128]{2,1,0:T(8,128)S(1)} %multiply_add_fusion.4), channel_id=1, source_target_pairs={{0,16},{8,24},{16,32},{24,40},{32,48},{40,56},{48,64},{56,72},{64,... | collective-permute-start | bytes 393224 | tf_op jit(solution)/shard_map/ppermute | solution.py:17
  38.2 3.8 %collective-permute-start.2 = (f32[16,16]{1,0:T(8,128)S(1)}, f32[16,16]{1,0:T(8,128)S(1)}, u32[]{:S(2)}, u32[]{:S(2)}) collective-permute-start(f32[16,16]{1,0:T(8,128)S(1)} %collective-permute-done.1), channel_id=1, source_target_pairs={{0,8},{8,16},{16,24},{24,32},{32,40},{40,48},{48,56},{56,64},{64,7... | collective-permute-start | bytes 3080 | tf_op jit(solution)/shard_map/ppermute | solution.py:17
  42.9 6.9 %collective-permute-start.9 = (f32[16,16,128]{2,1,0:T(8,128)S(1)}, f32[16,16,128]{2,1,0:T(8,128)S(1)}, u32[]{:S(2)}, u32[]{:S(2)}) collective-permute-start(f32[16,16,128]{2,1,0:T(8,128)S(1)} %multiply_add_fusion.3), channel_id=1, source_target_pairs={{0,32},{8,40},{16,48},{24,56},{32,64},{40,72},{48,80},{56,88},{64,... | collective-permute-start | bytes 393224 | tf_op jit(solution)/shard_map/ppermute | solution.py:17
  50.0 3.9 %collective-permute-start.3 = (f32[16,16]{1,0:T(8,128)S(1)}, f32[16,16]{1,0:T(8,128)S(1)}, u32[]{:S(2)}, u32[]{:S(2)}) collective-permute-start(f32[16,16]{1,0:T(8,128)S(1)} %mul.258), channel_id=1, source_target_pairs={{0,16},{8,24},{16,32},{24,40},{32,48},{40,56},{48,64},{56,72},{64,... | collective-permute-start | bytes 3080 | tf_op jit(solution)/shard_map/ppermute | solution.py:17
  54.6 9.5 %collective-permute-start.4 = (f32[16,16]{1,0:T(8,128)S(1)}, f32[16,16]{1,0:T(8,128)S(1)}, u32[]{:S(2)}, u32[]{:S(2)}) collective-permute-start(f32[16,16]{1,0:T(8,128)S(1)} %mul.259), channel_id=1, source_target_pairs={{0,32},{8,40},{16,48},{24,56},{32,64},{40,72},{48,80},{56,88},{64,... | collective-permute-start | bytes 3080 | tf_op jit(solution)/shard_map/ppermute | solution.py:17
  64.3 4.0 %collective-permute-start.10 = (f32[16,16,128]{2,1,0:T(8,128)S(1)}, f32[16,16,128]{2,1,0:T(8,128)S(1)}, u32[]{:S(2)}, u32[]{:S(2)}) collective-permute-start(f32[16,16,128]{2,1,0:T(8,128)S(1)} %multiply_add_fusion.2), channel_id=1, source_target_pairs={{0,64},{8,72},{16,80},{24,88},{32,96},{40,104},{48,112},{56,120},{... | collective-permute-start | bytes 393224 | tf_op jit(solution)/shard_map/ppermute | solution.py:17
  68.3 4.1 %select_convert_fusion = bf16[16,256,256]{2,1,0:T(8,128)(2,1)S(1)} fusion(pred[256,256]{1,0:T(8,128)(4,1)S(1)} %fusion.21, f32[256]{0:T(256)S(1)} %add_convert_fusion.2, f32[16,16]{1,0:T(8,128)S(1)} %bitcast.47, f32[16,16]{1,0:T(8,128)S(1)} %get-tuple-element.9, f32[16,16]{1,0:T(8,128)S(1)} %bitcast.48), kind=kOutput, calls=%fused_computation.1 | convolution fusion | flops 203620352 | bytes 2166784 | tf_op jit(solution)/shard_map/gtm,gms->gts/dot_general | solution.py:102
  72.4 4.0 %collective-permute-start.5 = (f32[16,16]{1,0:T(8,128)S(1)}, f32[16,16]{1,0:T(8,128)S(1)}, u32[]{:S(2)}, u32[]{:S(2)}) collective-permute-start(f32[16,16]{1,0:T(8,128)S(1)} %mul.260), channel_id=1, source_target_pairs={{0,64},{8,72},{16,80},{24,88},{32,96},{40,104},{48,112},{56,120},{... | collective-permute-start | bytes 3080 | tf_op jit(solution)/shard_map/ppermute | solution.py:17
  77.3 8.9 %collective-permute-start.11 = (f32[16,16,128]{2,1,0:T(8,128)S(1)}, f32[16,16,128]{2,1,0:T(8,128)S(1)}, u32[]{:S(2)}, u32[]{:S(2)}) collective-permute-start(f32[16,16,128]{2,1,0:T(8,128)S(1)} %multiply_add_fusion.1), channel_id=1, source_target_pairs={{0,128},{8,136},{16,144},{24,152},{32,160},{40,168},{48,176},{56,1... | collective-permute-start | bytes 393224 | tf_op jit(solution)/shard_map/ppermute | solution.py:17
  86.2 0.8 fusion.5
  87.0 1.1 collective-permute-done.11
  88.1 3.4 %fusion.3 = f32[16,128,256]{2,1,0:T(8,128)} fusion(f32[16,128,256]{2,1,0:T(8,128)S(1)} %fusion.5, f32[256]{0:T(256)S(1)} %get-tuple-element.10, f32[256]{0:T(256)S(1)} %add_convert_fusion.1, f32[16,16]{1,0:T(8,128)S(1)} %bitcast.49, f32[16,16,128]{2,1,0:T(8,128)S(1)} %multiply_add_fusion.1, f32[16,16,128]{2,1,0:T(8,128)S(1)} %collective-permute-done.11, ...), kind=kOutput, calls=%fused_computation.13 | convolution fusion | flops 102498304 | bytes 4461568 | tf_op jit(solution)/shard_map/tgm,gmc->tgc/dot_general | solution.py:113
  91.5 1.9 %copy.12 = f32[256,2048]{1,0:T(8,128)S(1)} copy(f32[256,2048]{0,1:T(8,128)} %bitcast.39) | data formatting | bytes 4194304 | tf_op jit(solution)/shard_map/convert_element_type | solution.py:116
  93.4 1.9 %multiply_reduce_fusion = f32[256]{0:T(256)S(1)} fusion(f32[256,2048]{1,0:T(8,128)S(1)} %copy.12, f32[3,256,2048]{2,1,0:T(8,128)} %copy-done), kind=kLoop, calls=%fused_computation.11 | loop fusion | flops 1572608 | bytes 4195328 | tf_op jit(solution)/shard_map/reduce_sum | solution.py:117
  95.3 3.1 %collective-permute-start.12 = (f32[256]{0:T(256)S(1)}, f32[256]{0:T(256)S(1)}, u32[]{:S(2)}, u32[]{:S(2)}) collective-permute-start(f32[256]{0:T(256)S(1)} %multiply_reduce_fusion), channel_id=1, source_target_pairs={{0,2},{2,0},{4,6},{6,4},{1,3},{3,1},{5,7},{7,5},{8,10},{10,8},{12,... | collective-permute-start | bytes 3080 | tf_op jit(solution)/shard_map/ppermute | solution.py:31
  98.5 1.2 collective-permute-done.12
  99.7 4.6 %collective-permute-start.13 = (f32[256]{0:T(256)S(1)}, f32[256]{0:T(256)S(1)}, u32[]{:S(2)}, u32[]{:S(2)}) collective-permute-start(f32[256]{0:T(256)S(1)} %add.103), channel_id=1, source_target_pairs={{0,4},{2,6},{4,0},{6,2},{1,5},{3,7},{5,1},{7,3},{8,12},{10,14},{12... | collective-permute-start | bytes 3080 | tf_op jit(solution)/shard_map/ppermute | solution.py:31
  104.3 1.2 collective-permute-done.13
  105.5 1.9 %multiply_convert_fusion = bf16[256,2048]{1,0:T(8,128)(2,1)S(1)} fusion(f32[2048]{0:T(1024)S(1)} %bitcast.50, f32[256]{0:T(256)S(1)} %add_rsqrt_fusion, f32[256,2048]{1,0:T(8,128)S(1)} %copy.12, f32[3,256,2048]{2,1,0:T(8,128)} %copy-done), kind=kLoop, calls=%fused_computation.10 | loop fusion | flops 2097152 | bytes 5252096 | tf_op jit(solution)/shard_map/convert_element_type | solution.py:120
  107.4 13.2 %collective-permute-start.14 = (bf16[256,2048]{1,0:T(8,128)(2,1)S(1)}, bf16[256,2048]{1,0:T(8,128)(2,1)S(1)}, u32[]{:S(2)}, u32[]{:S(2)}) collective-permute-start(bf16[256,2048]{1,0:T(8,128)(2,1)S(1)} %multiply_convert_fusion), channel_id=1, source_target_pairs={{0,1},{1,0},{2,3},{3,2},{4,5},{5,4},{6,7},{7,6},{8,9},{9,8},{10,11... | collective-permute-start | bytes 3145736 | tf_op jit(solution)/shard_map/ppermute | solution.py:23
  120.6 2.3 %collective-permute-done.14 = bf16[256,2048]{1,0:T(8,128)(2,1)S(1)} collective-permute-done((bf16[256,2048]{1,0:T(8,128)(2,1)S(1)}, bf16[256,2048]{1,0:T(8,128)(2,1)S(1)}, u32[]{:S(2)}, u32[]{:S(2)}) %collective-permute-start.14) | collective-permute-done | bytes 1048608 | tf_op jit(solution)/shard_map/ppermute | solution.py:23
  122.8 1.0 copy.29
  (45 shorter events, 7.7 us)
Async XLA Ops:
  0.9 8.6 %collective-permute-start = (bf16[3,2,2048]{2,1,0:T(2,128)(2,1)S(1)}, bf16[3,2,2048]{2,1,0:T(2,128)(2,1)S(1)}, u32[]{:S(2)}, u32[]{:S(2)}) collective-permute-start(bf16[3,2,2048]{2,1,0:T(2,128)(2,1)S(1)} %slice.42), channel_id=1, source_target_pairs={{0,8},{8,16},{16,24},{24,32},{32,40},{40,48},{48,56},{56,64},{64,7... | collective-permute-start | bytes 73736 | tf_op jit(solution)/shard_map/ppermute | solution.py:17
  15.9 2.6 %copy-start = (f32[3,256,2048]{2,1,0:T(8,128)}, f32[3,256,2048]{2,1,0:T(8,128)S(1)}, u32[]{:S(2)}) copy-start(f32[3,256,2048]{2,1,0:T(8,128)S(1)} %multiply_add_fusion) | copy-start | bytes 18874372
  15.9 12.2 %copy-start.1 = (f32[1,16,16]{2,1,0:T(8,128)S(1)}, f32[1,16,16]{2,1,0:T(8,128)}, u32[]{:S(2)}) copy-start(f32[1,16,16]{2,1,0:T(8,128)} %param.8) | copy-start | bytes 3076
  16.3 52.0 %copy-start.2 = (f32[1,16,16]{2,1,0:T(8,128)S(1)}, f32[1,16,16]{2,1,0:T(8,128)}, u32[]{:S(2)}) copy-start(f32[1,16,16]{2,1,0:T(8,128)} %param.9) | copy-start | bytes 3076
  19.3 5.1 %collective-permute-start.6 = (f32[16,16,128]{2,1,0:T(8,128)S(1)}, f32[16,16,128]{2,1,0:T(8,128)S(1)}, u32[]{:S(2)}, u32[]{:S(2)}) collective-permute-start(f32[16,16,128]{2,1,0:T(8,128)S(1)} %fusion.7), channel_id=1, source_target_pairs={{0,8},{8,16},{16,24},{24,32},{32,40},{40,48},{48,56},{56,64},{64,7... | collective-permute-start | bytes 393224 | tf_op jit(solution)/shard_map/ppermute | solution.py:17
  24.4 8.4 %collective-permute-start.7 = (f32[16,16,128]{2,1,0:T(8,128)S(1)}, f32[16,16,128]{2,1,0:T(8,128)S(1)}, u32[]{:S(2)}, u32[]{:S(2)}) collective-permute-start(f32[16,16,128]{2,1,0:T(8,128)S(1)} %collective-permute-done.6), channel_id=1, source_target_pairs={{0,8},{8,16},{16,24},{24,32},{32,40},{40,48},{48,56},{56,64},{64,7... | collective-permute-start | bytes 393224 | tf_op jit(solution)/shard_map/ppermute | solution.py:17
  28.2 4.6 %collective-permute-start.1 = (f32[16,16]{1,0:T(8,128)S(1)}, f32[16,16]{1,0:T(8,128)S(1)}, u32[]{:S(2)}, u32[]{:S(2)}) collective-permute-start(f32[16,16]{1,0:T(8,128)S(1)} %get-tuple-element.8), channel_id=1, source_target_pairs={{0,8},{8,16},{16,24},{24,32},{32,40},{40,48},{48,56},{56,64},{64,7... | collective-permute-start | bytes 3080 | tf_op jit(solution)/shard_map/ppermute | solution.py:17
  32.9 9.9 %collective-permute-start.8 = (f32[16,16,128]{2,1,0:T(8,128)S(1)}, f32[16,16,128]{2,1,0:T(8,128)S(1)}, u32[]{:S(2)}, u32[]{:S(2)}) collective-permute-start(f32[16,16,128]{2,1,0:T(8,128)S(1)} %multiply_add_fusion.4), channel_id=1, source_target_pairs={{0,16},{8,24},{16,32},{24,40},{32,48},{40,56},{48,64},{56,72},{64,... | collective-permute-start | bytes 393224 | tf_op jit(solution)/shard_map/ppermute | solution.py:17
  38.2 4.6 %collective-permute-start.2 = (f32[16,16]{1,0:T(8,128)S(1)}, f32[16,16]{1,0:T(8,128)S(1)}, u32[]{:S(2)}, u32[]{:S(2)}) collective-permute-start(f32[16,16]{1,0:T(8,128)S(1)} %collective-permute-done.1), channel_id=1, source_target_pairs={{0,8},{8,16},{16,24},{24,32},{32,40},{40,48},{48,56},{56,64},{64,7... | collective-permute-start | bytes 3080 | tf_op jit(solution)/shard_map/ppermute | solution.py:17
  42.9 21.2 %collective-permute-start.9 = (f32[16,16,128]{2,1,0:T(8,128)S(1)}, f32[16,16,128]{2,1,0:T(8,128)S(1)}, u32[]{:S(2)}, u32[]{:S(2)}) collective-permute-start(f32[16,16,128]{2,1,0:T(8,128)S(1)} %multiply_add_fusion.3), channel_id=1, source_target_pairs={{0,32},{8,40},{16,48},{24,56},{32,64},{40,72},{48,80},{56,88},{64,... | collective-permute-start | bytes 393224 | tf_op jit(solution)/shard_map/ppermute | solution.py:17
  50.0 4.7 %collective-permute-start.3 = (f32[16,16]{1,0:T(8,128)S(1)}, f32[16,16]{1,0:T(8,128)S(1)}, u32[]{:S(2)}, u32[]{:S(2)}) collective-permute-start(f32[16,16]{1,0:T(8,128)S(1)} %mul.258), channel_id=1, source_target_pairs={{0,16},{8,24},{16,32},{24,40},{32,48},{40,56},{48,64},{56,72},{64,... | collective-permute-start | bytes 3080 | tf_op jit(solution)/shard_map/ppermute | solution.py:17
  54.6 17.8 %collective-permute-start.4 = (f32[16,16]{1,0:T(8,128)S(1)}, f32[16,16]{1,0:T(8,128)S(1)}, u32[]{:S(2)}, u32[]{:S(2)}) collective-permute-start(f32[16,16]{1,0:T(8,128)S(1)} %mul.259), channel_id=1, source_target_pairs={{0,32},{8,40},{16,48},{24,56},{32,64},{40,72},{48,80},{56,88},{64,... | collective-permute-start | bytes 3080 | tf_op jit(solution)/shard_map/ppermute | solution.py:17
  64.3 13.0 %collective-permute-start.10 = (f32[16,16,128]{2,1,0:T(8,128)S(1)}, f32[16,16,128]{2,1,0:T(8,128)S(1)}, u32[]{:S(2)}, u32[]{:S(2)}) collective-permute-start(f32[16,16,128]{2,1,0:T(8,128)S(1)} %multiply_add_fusion.2), channel_id=1, source_target_pairs={{0,64},{8,72},{16,80},{24,88},{32,96},{40,104},{48,112},{56,120},{... | collective-permute-start | bytes 393224 | tf_op jit(solution)/shard_map/ppermute | solution.py:17
  72.4 4.8 %collective-permute-start.5 = (f32[16,16]{1,0:T(8,128)S(1)}, f32[16,16]{1,0:T(8,128)S(1)}, u32[]{:S(2)}, u32[]{:S(2)}) collective-permute-start(f32[16,16]{1,0:T(8,128)S(1)} %mul.260), channel_id=1, source_target_pairs={{0,64},{8,72},{16,80},{24,88},{32,96},{40,104},{48,112},{56,120},{... | collective-permute-start | bytes 3080 | tf_op jit(solution)/shard_map/ppermute | solution.py:17
  77.3 10.8 %collective-permute-start.11 = (f32[16,16,128]{2,1,0:T(8,128)S(1)}, f32[16,16,128]{2,1,0:T(8,128)S(1)}, u32[]{:S(2)}, u32[]{:S(2)}) collective-permute-start(f32[16,16,128]{2,1,0:T(8,128)S(1)} %multiply_add_fusion.1), channel_id=1, source_target_pairs={{0,128},{8,136},{16,144},{24,152},{32,160},{40,168},{48,176},{56,1... | collective-permute-start | bytes 393224 | tf_op jit(solution)/shard_map/ppermute | solution.py:17
  93.4 12.0 %copy-start.3 = (f32[1,2048]{1,0:T(1,128)S(1)}, f32[1,2048]{1,0:T(1,128)}, u32[]{:S(2)}) copy-start(f32[1,2048]{1,0:T(1,128)} %param.10) | copy-start | bytes 24580
  95.3 4.3 %collective-permute-start.12 = (f32[256]{0:T(256)S(1)}, f32[256]{0:T(256)S(1)}, u32[]{:S(2)}, u32[]{:S(2)}) collective-permute-start(f32[256]{0:T(256)S(1)} %multiply_reduce_fusion), channel_id=1, source_target_pairs={{0,2},{2,0},{4,6},{6,4},{1,3},{3,1},{5,7},{7,5},{8,10},{10,8},{12,... | collective-permute-start | bytes 3080 | tf_op jit(solution)/shard_map/ppermute | solution.py:31
  99.7 5.8 %collective-permute-start.13 = (f32[256]{0:T(256)S(1)}, f32[256]{0:T(256)S(1)}, u32[]{:S(2)}, u32[]{:S(2)}) collective-permute-start(f32[256]{0:T(256)S(1)} %add.103), channel_id=1, source_target_pairs={{0,4},{2,6},{4,0},{6,2},{1,5},{3,7},{5,1},{7,3},{8,12},{10,14},{12... | collective-permute-start | bytes 3080 | tf_op jit(solution)/shard_map/ppermute | solution.py:31
  107.4 15.5 %collective-permute-start.14 = (bf16[256,2048]{1,0:T(8,128)(2,1)S(1)}, bf16[256,2048]{1,0:T(8,128)(2,1)S(1)}, u32[]{:S(2)}, u32[]{:S(2)}) collective-permute-start(bf16[256,2048]{1,0:T(8,128)(2,1)S(1)} %multiply_convert_fusion), channel_id=1, source_target_pairs={{0,1},{1,0},{2,3},{3,2},{4,5},{5,4},{6,7},{7,6},{8,9},{9,8},{10,11... | collective-permute-start | bytes 3145736 | tf_op jit(solution)/shard_map/ppermute | solution.py:23
